TPU v7x, 32 devices: a whole 2x2x4 slice. The times are simulated.
32 devices in a mesh: section: 2 (over x), fsdp: 4 (over z), dp: 4 (over y, core).
Axes of the slice: x: 2, y: 2, z: 4, core: 2. Of those that a mesh axis runs over, the one named last changes fastest.
Arguments:
- activations: bfloat16 [2, 4, 512, 3584], P('section', None, ('fsdp', 'dp')), may hold values from -6 to 6
- out_grad: bfloat16 [2, 4, 512, 14336], P('section', None, ('fsdp', 'dp')), may hold values from -6 to 6
- blocks: bfloat16 [2, 16, 128, 128], P('section', 'fsdp'), may hold values from -0.5 to 0.5
- pattern: int32 [2, 16, 2], P('section', 'fsdp'), may hold values from 0 to 111, as said below
- order: int32 [4], replicated, may hold values from 0 to 3, each once
Outputs:
- received: bfloat16 [2, 4, 512, 3584], P('section', None, ('fsdp', 'dp'))
- weight_grad: float32 [2, 16, 128, 128], P('section', 'fsdp')
Inputs may be any that keep to these rules, and one draw needn't show every extreme that they name: pattern[s, b, 0] < 28 and pattern[s, b, 1] < 112; no two blocks of one section share both indices; within a section the blocks stand in ascending order of (row, column). `order`: a permutation of the microbatches.
All inputs are finite; a program needn't handle non-finite values.
Results may differ from a plain program's by a relative error of at most 0.0049.
Values may be sent and summed in bfloat16 or wider, within the bound.
No kernel may reach another device: no remote copies, remote signals or barrier semaphores. Data moves between devices by JAX's collectives and lax.ppermute only.
A program may use at most 128 MiB of HBM per device.

v0:
```python
import math
import jax
import jax.numpy as jnp
from jax import lax
from jax.sharding import PartitionSpec as P


def passed_along(block, axis, distance):
    devices = range(lax.axis_size(axis))
    route = [(i - distance, i) for i in devices if i - distance in devices]
    return lax.ppermute(block, axis, route)


def silu_slope(pre_act):
    sigmoid_val = jax.nn.sigmoid(pre_act)
    return sigmoid_val * (1.0 + pre_act * (1.0 - sigmoid_val))


def in_groups(step_fn, running, shard_blocks, first_block):
    block_count = shard_blocks.shape[0]
    group_size = math.gcd(block_count, 32)
    if group_size == block_count:
        return step_fn(running, shard_blocks, first_block)

    def one_group(number, carried):
        segment = lax.dynamic_slice_in_dim(shard_blocks, number * group_size, group_size, 0)
        return step_fn(carried, segment, first_block + number * group_size)

    return lax.fori_loop(0, block_count // group_size, one_group, running)


def local(activations, out_grad, blocks, pattern, order):
    block_size = blocks.shape[-1]
    micro_count = activations.shape[1]
    tok_rows = activations.shape[1] * activations.shape[2]
    row_count = activations.shape[3] // block_size
    col_count = out_grad.shape[3] // block_size
    features = activations[0].reshape(tok_rows, row_count, block_size)
    hidden_grad = out_grad[0].reshape(tok_rows, out_grad.shape[3])
    own_blocks = blocks[0]
    all_indices = lax.all_gather(pattern[0], "fsdp", axis=0, tiled=True)

    def forward_step(running, shard_blocks, first_block):
        indices = lax.dynamic_slice_in_dim(all_indices, first_block, shard_blocks.shape[0], 0)
        rows_in = jnp.take(features, indices[:, 0], axis=1)
        product = jnp.einsum(
            "tbk,bkn->tbn", rows_in, shard_blocks, preferred_element_type=jnp.float32
        )
        return running.at[:, indices[:, 1]].add(product)

    pre_zero = jnp.zeros((tok_rows, col_count, block_size), jnp.float32)
    pre_act = in_groups(
        forward_step, pre_zero, lax.all_gather(own_blocks, "fsdp", axis=0, tiled=True), jnp.int32(0)
    )
    act_grad = (hidden_grad.astype(jnp.float32) * silu_slope(pre_act.reshape(tok_rows, -1))).astype(
        jnp.bfloat16
    )
    grad_cols = act_grad.reshape(tok_rows, col_count, block_size)

    def backward_step(running, shard_blocks, first_block):
        indices = lax.dynamic_slice_in_dim(all_indices, first_block, shard_blocks.shape[0], 0)
        cols_in = jnp.take(grad_cols, indices[:, 1], axis=1)
        product = jnp.einsum(
            "tbn,bkn->tbk", cols_in, shard_blocks, preferred_element_type=jnp.float32
        )
        return running.at[:, indices[:, 0]].add(product)

    back_zero = jnp.zeros((tok_rows, row_count, block_size), jnp.float32)
    input_grad = in_groups(
        backward_step,
        back_zero,
        lax.all_gather(own_blocks, "fsdp", axis=0, tiled=True),
        jnp.int32(0),
    )
    input_grad = input_grad.astype(jnp.bfloat16).reshape(
        micro_count, activations.shape[2], activations.shape[3]
    )
    ordered = jnp.take(input_grad, order, axis=0)
    received = passed_along(ordered, "section", -1)
    indices = all_indices
    rows_in = jnp.take(features, indices[:, 0], axis=1)
    cols_in = jnp.take(grad_cols, indices[:, 1], axis=1)
    owned_grads = lax.psum_scatter(
        jnp.einsum("tbk,tbn->bkn", rows_in, cols_in, preferred_element_type=jnp.float32),
        "fsdp",
        scatter_dimension=0,
        tiled=True,
    )
    summed = lax.psum(owned_grads, "dp")
    grad_scale = 1.0 / math.sqrt(tok_rows * lax.axis_size("fsdp") * lax.axis_size("dp"))
    return (received[None], (summed * grad_scale)[None])


def solution(mesh):
    in_specs = (
        P("section", None, ("fsdp", "dp"), None),
        P("section", None, ("fsdp", "dp"), None),
        P("section", "fsdp", None, None),
        P("section", "fsdp", None),
        P(),
    )
    out_specs = (P("section", None, ("fsdp", "dp"), None), P("section", "fsdp", None, None))
    return jax.shard_map(local, mesh=mesh, in_specs=in_specs, out_specs=out_specs, check_vma=False)
```

profile of v0, /device:TPU:0, one launch (start us, length us, event | category | flops | bytes accessed | tf_op | source)
XLA Modules:
  0.0 135.6 jit_solution(16365849403868641486)
XLA Ops:
  7.2 0.0 reduce-scatter.2.cloned.1.call-start
  7.2 0.8 copy.12
  8.0 13.6 %all-gather = s32[1,16,2]{2,0,1:T(1,128)S(1)} all-gather(s32[1,4,2]{2,0,1:T(1,128)S(1)} %copy.12), channel_id=2, replica_groups=mesh['section'=2,'fsdp'=4,'dp'=4] {'fsdp'}, dimensions={1}, use_global_device_ids=true | all-gather | bytes 160 | tf_op jit(solution)/shard_map/all_gather | solution.py:41
  21.6 0.1 copy.13
  21.7 1.6 %reshape_squeeze.4 = bf16[128,28,128]{2,1,0:T(8,128)(2,1)S(1)} reshape(bf16[1,4,32,3584]{3,2,1,0:T(8,128)(2,1)} %param.9) | data formatting | bytes 1835008 | tf_op jit(solution)/shard_map/reshape;squeeze | solution.py:38
  23.3 0.4 copy.14
  23.7 16.1 %all-gather.1 = bf16[1,16,128,128]{3,2,0,1:T(8,128)(2,1)S(1)} all-gather(bf16[1,4,128,128]{3,2,0,1:T(8,128)(2,1)} %bitcast.40), channel_id=3, replica_groups=mesh['section'=2,'fsdp'=4,'dp'=4] {'fsdp'}, dimensions={1}, use_global_device_ids=true | all-gather | bytes 655360 | tf_op jit(solution)/shard_map/all_gather | solution.py:72
  39.8 5.9 %copy.20 = f32[16,8,112,128]{3,2,1,0:T(8,128)} copy(bf16[16,8,112,128]{3,1,2,0:T(8,128)(2,1)} %bitcast.38) | data formatting | bytes 11010048
  45.7 0.6 gather_fusion.1
  46.3 0.4 fusion.6
  46.7 3.9 %broadcast_in_dim.46 = f32[128,112,128]{2,0,1:T(8,128)} broadcast(f32[]{:T(128)} %constant.23.clone.1), dimensions={} | broadcast | bytes 7340036 | tf_op jit(solution)/shard_map/broadcast_in_dim | solution.py:51
  50.6 3.4 %scatter_fusion = f32[128,112,128]{2,0,1:T(8,128)} fusion(f32[128,112,128]{2,0,1:T(8,128)} %broadcast_in_dim.46, s32[16]{0:T(128)S(1)} %get-tuple-element.10, f32[16,128,128]{2,1,0:T(8,128)S(1)} %fusion.6), kind=kCustom, calls=%fused_computation.3 | custom fusion | flops 262144 | bytes 3145792 | tf_op jit(solution)/shard_map/scatter-add | solution.py:49
  54.0 0.0 copy-start
  54.0 8.4 %fusion = bf16[128,112,128]{2,0,1:T(8,128)(2,1)} fusion(f32[128,112,128]{2,1,0:T(8,128)} %bitcast.37, f32[128,112,128]{2,0,1:T(8,128)} %scatter_fusion), kind=kLoop, calls=%fused_computation.6 | loop fusion | flops 16515072 | bytes 18350080 | tf_op jit(solution)/shard_map/convert_element_type | solution.py:55
  62.4 2.7 %gather_fusion.2 = bf16[16,128,128]{2,1,0:T(8,128)(2,1)S(1)} fusion(bf16[128,112,128]{2,0,1:T(8,128)(2,1)} %fusion, s32[1024]{0:T(1024)S(1)} %get-tuple-element.12), kind=kCustom, calls=%fused_computation.1.clone | custom fusion | bytes 1048640 | tf_op jit(solution)/shard_map/jit(_take)/gather | solution.py:62
  65.1 1.4 %fusion.1 = f32[16,128,128]{2,1,0:T(8,128)} fusion(bf16[16,128,128]{2,1,0:T(8,128)(2,1)S(1)} %gather_fusion.1, pred[16]{0:T(512)(128)(4,1)S(1)} %get-tuple-element.8, bf16[16,128,128]{2,1,0:T(8,128)(2,1)S(1)} %gather_fusion.2, pred[16]{0:T(512)(128)(4,1)S(1)} %get-tuple-element.4), kind=kOutput, calls=%fused_computation.8 | convolution fusion | flops 67633152 | bytes 2097184 | tf_op jit(solution)/shard_map/tbk,tbn->bkn/dot_general | solution.py:84
  66.5 0.0 reduce-scatter.2.cloned.1.call-update
  66.6 0.0 all-reduce.2.cloned.1.call-start
  66.6 0.5 fusion.3
  67.1 0.0 copy-done
  67.2 0.2 broadcast_in_dim.45
  67.4 1.6 %scatter_fusion.1 = f32[128,28,128]{2,0,1:T(8,128)S(1)} fusion(f32[128,28,128]{2,0,1:T(8,128)S(1)} %broadcast_in_dim.45, s32[16]{0:T(128)S(1)} %get-tuple-element.11, f32[16,128,128]{2,1,0:T(8,128)S(1)} %fusion.3), kind=kCustom, calls=%fused_computation.4 | custom fusion | flops 262144 | bytes 3145792 | tf_op jit(solution)/shard_map/scatter-add | solution.py:66
  69.0 0.1 convert_element_type.17
  69.1 0.6 copy.17
  69.8 0.5 reshape.27
  70.3 0.6 gather_fusion
  70.9 0.2 broadcast_select_fusion
  71.1 1.3 collective-permute-start
  72.4 20.7 %reduce-scatter.2.cloned.1.call-done = f32[4,128,128]{2,1,0:T(8,128)} async-done(((f32[16,128,128]{2,1,0:T(8,128)}), f32[4,128,128]{2,1,0:T(8,128)}) %reduce-scatter.2.cloned.1.call-update) | async-done | bytes 262160 | tf_op jit(solution)/shard_map/reduce_scatter | solution.py:83
  93.0 0.0 all-reduce.2.cloned.1.call-update
  93.1 0.0 collective-permute-done
  93.1 33.1 %all-reduce.2.cloned.1.call-done = f32[4,128,128]{2,1,0:T(8,128)} async-done(((f32[4,128,128]{2,1,0:T(8,128)}), f32[4,128,128]{2,1,0:T(8,128)}) %all-reduce.2.cloned.1.call-update) | async-done | bytes 262160 | tf_op jit(solution)/shard_map/psum | solution.py:89
  126.2 1.7 %multiply_bitcast_fusion = f32[1,4,128,128]{3,2,1,0:T(8,128)} fusion(f32[4,128,128]{2,1,0:T(8,128)} %all-reduce.2.cloned.1.call-done), kind=kLoop, calls=%fused_computation.19 | loop fusion | flops 65536 | bytes 524288 | tf_op jit(solution)/shard_map/broadcast_in_dim | solution.py:91
  127.9 0.9 copy.28
  (6 shorter events, 0.0 us)
Async XLA Ops:
  7.2 85.9 %reduce-scatter.2.cloned.1.call-start = ((), (), s32[]{:S(2)}) async-start(), calls=%async_computation.1 | async-start | bytes 1310720 | tf_op jit(solution)/shard_map/reduce_scatter | solution.py:83
  54.0 13.1 %copy-start = (s32[4]{0:T(128)S(1)}, s32[4]{0:T(128)}, u32[]{:S(2)}) copy-start(s32[4]{0:T(128)} %param.13) | copy-start | bytes 52
  66.6 59.6 %all-reduce.2.cloned.1.call-start = ((), (), s32[]{:S(2)}) async-start(), calls=%async_computation.2 | async-start | bytes 524288 | tf_op jit(solution)/shard_map/psum | solution.py:89
  71.1 22.0 %collective-permute-start = (bf16[4,32,3584]{2,1,0:T(8,128)(2,1)S(1)}, bf16[4,32,3584]{2,1,0:T(8,128)(2,1)S(1)}, u32[]{:S(2)}, u32[]{:S(2)}) collective-permute-start(bf16[4,32,3584]{2,1,0:T(8,128)(2,1)S(1)} %broadcast_select_fusion), channel_id=1, source_target_pairs={{16,0},{17,1},{18,2},{19,3},{20,4},{21,5},{22,6},{23,7},{24,8},{25... | collective-permute-start | bytes 2752520 | tf_op jit(solution)/shard_map/ppermute | solution.py:11
Sparse Core Ops, SparseCore 0:
  66.7 26.2 reduce-scatter.1
  95.4 30.7 all-reduce.1
where the time goes:
time: 136 us
  waiting for transfers between devices  53.8 us (40%)
  blocking collectives  29.7 us (22%)
  local copies, waits for them, and re-layouts  18.8 us (14%)
  other arithmetic  15.4 us (11%)
  between operations  14.2 us (10%)
  matrix products  2.29 us (2%)
  starting transfers between devices  1.37 us (1%)
    psum x1, waiting for transfers between devices, local(): summed = lax.psum(owned_grads, 'dp')  33.1 us
    reduce_scatter x1, waiting for transfers between devices, local(): lax.psum_scatter(jnp.einsum('tbk,tbn->bkn', rows_in, cols_in, preferred_e...  20.7 us
    all_gather x1, blocking collectives, local(): lax.all_gather(own_blocks, 'fsdp', axis=0, tiled=True)  16.1 us
    all_gather x1, blocking collectives, local(): all_indices = lax.all_gather(pattern[0], 'fsdp', axis=0, tiled=True)  13.6 us
    convert_element_type x1, other arithmetic, local(): (hidden_grad.astype(jnp.float32) * silu_slope(pre_act.reshape(tok_rows, -...  8.43 us
    unnamed x5, local copies, waits for them, and re-layouts  7.54 us
    broadcast_in_dim x1, local copies, waits for them, and re-layouts, local(): pre_zero = jnp.zeros((tok_rows, col_count, block_size), jnp.float32)  3.95 us
    scatter-add x1, other arithmetic, forward_step(): return running.at[:, indices[:, 1]].add(product)  3.38 us
  transfers between devices with their start and end apart: 3, of which 2 were waited for; matrix products, arithmetic and copies ran while one was open for 3% of the time, Pallas kernels for 0%

commit v1 on v0

--- a/solution.py
+++ b/solution.py
@@ -3,6 +3,12 @@
 import jax.numpy as jnp
 from jax import lax
 from jax.sharding import PartitionSpec as P
+
+
+def laid_out(parts, dim):
+    parts = jnp.moveaxis(parts, 0, dim)
+    dims = parts.shape
+    return parts.reshape(*dims[:dim], dims[dim] * dims[dim + 1], *dims[dim + 2 :])
 
 
 def passed_along(block, axis, distance):
@@ -38,7 +44,14 @@
     features = activations[0].reshape(tok_rows, row_count, block_size)
     hidden_grad = out_grad[0].reshape(tok_rows, out_grad.shape[3])
     own_blocks = blocks[0]
-    all_indices = lax.all_gather(pattern[0], "fsdp", axis=0, tiled=True)
+    length = lax.axis_size("fsdp")
+    right = [(i_2, (i_2 + 1) % length) for i_2 in range(length)]
+    blocks_2 = [pattern[0]]
+    while len(blocks_2) < length:
+        blocks_2.append(lax.ppermute(blocks_2[-1], "fsdp", right))
+    index = lax.axis_index("fsdp")
+    blocks_2 = jnp.stack(blocks_2)[(index - jnp.arange(length)) % length]
+    all_indices = laid_out(blocks_2, 0)
 
     def forward_step(running, shard_blocks, first_block):
         indices = lax.dynamic_slice_in_dim(all_indices, first_block, shard_blocks.shape[0], 0)

time: 136 us -> 136 us (level)
  blocking collectives: 29.7 us -> 15.6 us
  waiting for transfers between devices: 53.8 us -> 63.5 us
  starting transfers between devices: 1.37 us -> 4.82 us
  other arithmetic: 15.4 us -> 16.8 us
    all_gather x1 -> x0, blocking collectives: 13.6 us -> none  [local(): all_indices = lax.all_gather(pattern[0], 'fsdp', axis=0, tiled=True)]
    ppermute x0 -> x3, waiting for transfers between devices: none -> 10.4 us  [local(): blocks_2.append(lax.ppermute(blocks_2[-1], 'fsdp', right))]
    ppermute x0 -> x3, starting transfers between devices: none -> 3.45 us  [local(): blocks_2.append(lax.ppermute(blocks_2[-1], 'fsdp', right))]
    unnamed x5 -> x4, local copies, waits for them, and re-layouts: 7.54 us -> 6.76 us
  transfers between devices with their start and end apart: 3 -> 6, of which waited for: 2 -> 4; matrix products, arithmetic and copies ran while one was open for 3% -> 10% of each run, Pallas kernels for 0% -> 0%
where the time goes in v1:
time: 136 us
  waiting for transfers between devices  63.5 us (47%)
  local copies, waits for them, and re-layouts  18.6 us (14%)
  other arithmetic  16.8 us (12%)
  blocking collectives  15.6 us (11%)
  between operations  14.2 us (10%)
  starting transfers between devices  4.82 us (4%)
  matrix products  2.27 us (2%)
    psum x1, waiting for transfers between devices, local(): summed = lax.psum(owned_grads, 'dp')  33.1 us
    reduce_scatter x1, waiting for transfers between devices, local(): lax.psum_scatter(jnp.einsum('tbk,tbn->bkn', rows_in, cols_in, preferred_e...  19.9 us
    all_gather x1, blocking collectives, local(): lax.all_gather(own_blocks, 'fsdp', axis=0, tiled=True)  15.6 us
    ppermute x3, waiting for transfers between devices, local(): blocks_2.append(lax.ppermute(blocks_2[-1], 'fsdp', right))  10.4 us
    convert_element_type x1, other arithmetic, local(): (hidden_grad.astype(jnp.float32) * silu_slope(pre_act.reshape(tok_rows, -...  8.44 us
    unnamed x4, local copies, waits for them, and re-layouts  6.76 us
    broadcast_in_dim x1, local copies, waits for them, and re-layouts, local(): pre_zero = jnp.zeros((tok_rows, col_count, block_size), jnp.float32)  3.93 us
    ppermute x3, starting transfers between devices, local(): blocks_2.append(lax.ppermute(blocks_2[-1], 'fsdp', right))  3.45 us
  transfers between devices with their start and end apart: 6, of which 4 were waited for; matrix products, arithmetic and copies ran while one was open for 10% of the time, Pallas kernels for 0%

profile of v1, /device:TPU:0, one launch (start us, length us, event | category | flops | bytes accessed | tf_op | source)
XLA Modules:
  0.0 135.7 jit_solution(155801294314059352)
XLA Ops:
  7.2 0.0 reduce-scatter.2.cloned.1.call-start
  7.2 3.1 %collective-permute-start = (s32[4,2]{0,1:T(2,128)}, s32[4,2]{0,1:T(2,128)S(1)}, u32[]{:S(2)}, u32[]{:S(2)}) collective-permute-start(s32[4,2]{0,1:T(2,128)} %bitcast.48), channel_id=1, source_target_pairs={{0,4},{4,8},{8,12},{12,0},{1,5},{5,9},{9,13},{13,1},{2,6},{6,10},{... | collective-permute-start | bytes 104 | tf_op jit(solution)/shard_map/ppermute | solution.py:51
  10.3 0.7 compare_select_fusion.5
  11.0 0.7 compare_and_fusion.2
  11.7 0.0 copy-start
  11.7 1.6 %reshape_squeeze.4 = bf16[128,28,128]{2,1,0:T(8,128)(2,1)S(1)} reshape(bf16[1,4,32,3584]{3,2,1,0:T(8,128)(2,1)} %param.9) | data formatting | bytes 1835008 | tf_op jit(solution)/shard_map/reshape;squeeze | solution.py:44
  13.3 0.4 copy.15
  13.7 15.6 %all-gather = bf16[1,16,128,128]{3,2,0,1:T(8,128)(2,1)S(1)} all-gather(bf16[1,4,128,128]{3,2,0,1:T(8,128)(2,1)} %bitcast.47), channel_id=2, replica_groups=mesh['section'=2,'fsdp'=4,'dp'=4] {'fsdp'}, dimensions={1}, use_global_device_ids=true | all-gather | bytes 655360 | tf_op jit(solution)/shard_map/all_gather | solution.py:85
  29.2 5.8 %copy.21 = f32[16,8,112,128]{3,2,1,0:T(8,128)} copy(bf16[16,8,112,128]{3,1,2,0:T(8,128)(2,1)} %bitcast.45) | data formatting | bytes 11010048
  35.1 0.0 collective-permute-done
  35.1 0.3 collective-permute-start.1
  35.4 5.0 %collective-permute-done.1 = s32[4,2]{0,1:T(2,128)S(1)} collective-permute-done((s32[4,2]{0,1:T(2,128)S(1)}, s32[4,2]{0,1:T(2,128)S(1)}, u32[]{:S(2)}, u32[]{:S(2)}) %collective-permute-start.1) | collective-permute-done | bytes 64 | tf_op jit(solution)/shard_map/ppermute | solution.py:51
  40.5 0.0 collective-permute-start.2
  40.5 5.4 %collective-permute-done.2 = s32[4,2]{0,1:T(2,128)S(1)} collective-permute-done((s32[4,2]{0,1:T(2,128)S(1)}, s32[4,2]{0,1:T(2,128)S(1)}, u32[]{:S(2)}, u32[]{:S(2)}) %collective-permute-start.2) | collective-permute-done | bytes 64 | tf_op jit(solution)/shard_map/ppermute | solution.py:51
  45.8 0.0 copy-done
  45.8 0.6 gather_fusion
  46.4 0.1 reshape.79
  46.5 0.6 gather_fusion.2
  47.2 0.4 fusion.6
  47.6 3.9 %broadcast_in_dim.47 = f32[128,112,128]{2,0,1:T(8,128)} broadcast(f32[]{:T(128)} %constant.42.clone.1), dimensions={} | broadcast | bytes 7340036 | tf_op jit(solution)/shard_map/broadcast_in_dim | solution.py:64
  51.5 3.4 %scatter_fusion = f32[128,112,128]{2,0,1:T(8,128)} fusion(f32[128,112,128]{2,0,1:T(8,128)} %broadcast_in_dim.47, s32[16]{0:T(128)S(1)} %get-tuple-element.10, f32[16,128,128]{2,1,0:T(8,128)S(1)} %fusion.6), kind=kCustom, calls=%fused_computation.4 | custom fusion | flops 262144 | bytes 3145792 | tf_op jit(solution)/shard_map/scatter-add | solution.py:62
  54.9 8.4 %fusion = bf16[128,112,128]{2,0,1:T(8,128)(2,1)} fusion(f32[128,112,128]{2,1,0:T(8,128)} %bitcast.44, f32[128,112,128]{2,0,1:T(8,128)} %scatter_fusion), kind=kLoop, calls=%fused_computation.7 | loop fusion | flops 16515072 | bytes 18350080 | tf_op jit(solution)/shard_map/convert_element_type | solution.py:68
  63.3 2.7 %gather_fusion.3 = bf16[16,128,128]{2,1,0:T(8,128)(2,1)S(1)} fusion(bf16[128,112,128]{2,0,1:T(8,128)(2,1)} %fusion, s32[1024]{0:T(1024)S(1)} %get-tuple-element.12), kind=kCustom, calls=%fused_computation.1.clone | custom fusion | bytes 1048640 | tf_op jit(solution)/shard_map/jit(_take)/gather | solution.py:75
  66.0 1.4 %fusion.1 = f32[16,128,128]{2,1,0:T(8,128)} fusion(bf16[16,128,128]{2,1,0:T(8,128)(2,1)S(1)} %gather_fusion.2, pred[16]{0:T(512)(128)(4,1)S(1)} %get-tuple-element.8, bf16[16,128,128]{2,1,0:T(8,128)(2,1)S(1)} %gather_fusion.3, pred[16]{0:T(512)(128)(4,1)S(1)} %get-tuple-element.4), kind=kOutput, calls=%fused_computation.9 | convolution fusion | flops 67633152 | bytes 2097184 | tf_op jit(solution)/shard_map/tbk,tbn->bkn/dot_general | solution.py:97
  67.4 0.0 reduce-scatter.2.cloned.1.call-update
  67.4 0.0 all-reduce.2.cloned.1.call-start
  67.5 0.5 fusion.3
  68.0 0.2 broadcast_in_dim.46
  68.2 1.6 %scatter_fusion.1 = f32[128,28,128]{2,0,1:T(8,128)S(1)} fusion(f32[128,28,128]{2,0,1:T(8,128)S(1)} %broadcast_in_dim.46, s32[16]{0:T(128)S(1)} %get-tuple-element.11, f32[16,128,128]{2,1,0:T(8,128)S(1)} %fusion.3), kind=kCustom, calls=%fused_computation.5 | custom fusion | flops 262144 | bytes 3145792 | tf_op jit(solution)/shard_map/scatter-add | solution.py:79
  69.8 0.1 convert_element_type.17
  70.0 0.6 copy.18
  70.6 0.5 reshape.80
  71.1 0.6 gather_fusion.1
  71.7 0.2 broadcast_select_fusion
  71.9 1.3 collective-permute-start.3
  73.2 19.9 %reduce-scatter.2.cloned.1.call-done = f32[4,128,128]{2,1,0:T(8,128)} async-done(((f32[16,128,128]{2,1,0:T(8,128)}), f32[4,128,128]{2,1,0:T(8,128)}) %reduce-scatter.2.cloned.1.call-update) | async-done | bytes 262160 | tf_op jit(solution)/shard_map/reduce_scatter | solution.py:96
  93.1 0.0 all-reduce.2.cloned.1.call-update
  93.1 0.0 collective-permute-done.3
  93.1 33.1 %all-reduce.2.cloned.1.call-done = f32[4,128,128]{2,1,0:T(8,128)} async-done(((f32[4,128,128]{2,1,0:T(8,128)}), f32[4,128,128]{2,1,0:T(8,128)}) %all-reduce.2.cloned.1.call-update) | async-done | bytes 262160 | tf_op jit(solution)/shard_map/psum | solution.py:102
  126.3 1.7 %multiply_bitcast_fusion = f32[1,4,128,128]{3,2,1,0:T(8,128)} fusion(f32[4,128,128]{2,1,0:T(8,128)} %all-reduce.2.cloned.1.call-done), kind=kLoop, calls=%fused_computation.20 | loop fusion | flops 65536 | bytes 524288 | tf_op jit(solution)/shard_map/broadcast_in_dim | solution.py:104
  127.9 0.9 copy.29
  (8 shorter events, 0.1 us)
Async XLA Ops:
  7.2 85.9 %reduce-scatter.2.cloned.1.call-start = ((), (), s32[]{:S(2)}) async-start(), calls=%async_computation.1 | async-start | bytes 1310720 | tf_op jit(solution)/shard_map/reduce_scatter | solution.py:96
  7.2 27.9 %collective-permute-start = (s32[4,2]{0,1:T(2,128)}, s32[4,2]{0,1:T(2,128)S(1)}, u32[]{:S(2)}, u32[]{:S(2)}) collective-permute-start(s32[4,2]{0,1:T(2,128)} %bitcast.48), channel_id=1, source_target_pairs={{0,4},{4,8},{8,12},{12,0},{1,5},{5,9},{9,13},{13,1},{2,6},{6,10},{... | collective-permute-start | bytes 104 | tf_op jit(solution)/shard_map/ppermute | solution.py:51
  11.7 34.2 %copy-start = (s32[1,4,2]{1,2,0:T(2,128)S(1)}, s32[1,4,2]{1,2,0:T(2,128)}, u32[]{:S(2)}) copy-start(s32[1,4,2]{1,2,0:T(2,128)} %param.12) | copy-start | bytes 100
  35.1 5.4 %collective-permute-start.1 = (s32[4,2]{0,1:T(2,128)S(1)}, s32[4,2]{0,1:T(2,128)S(1)}, u32[]{:S(2)}, u32[]{:S(2)}) collective-permute-start(s32[4,2]{0,1:T(2,128)S(1)} %collective-permute-done), channel_id=1, source_target_pairs={{0,4},{4,8},{8,12},{12,0},{1,5},{5,9},{9,13},{13,1},{2,6},{6,10},{... | collective-permute-start | bytes 104 | tf_op jit(solution)/shard_map/ppermute | solution.py:51
  40.5 5.4 %collective-permute-start.2 = (s32[4,2]{0,1:T(2,128)S(1)}, s32[4,2]{0,1:T(2,128)S(1)}, u32[]{:S(2)}, u32[]{:S(2)}) collective-permute-start(s32[4,2]{0,1:T(2,128)S(1)} %collective-permute-done.1), channel_id=1, source_target_pairs={{0,4},{4,8},{8,12},{12,0},{1,5},{5,9},{9,13},{13,1},{2,6},{6,10},{... | collective-permute-start | bytes 104 | tf_op jit(solution)/shard_map/ppermute | solution.py:51
  67.4 58.8 %all-reduce.2.cloned.1.call-start = ((), (), s32[]{:S(2)}) async-start(), calls=%async_computation.2 | async-start | bytes 524288 | tf_op jit(solution)/shard_map/psum | solution.py:102
  71.9 21.3 %collective-permute-start.3 = (bf16[4,32,3584]{2,1,0:T(8,128)(2,1)S(1)}, bf16[4,32,3584]{2,1,0:T(8,128)(2,1)S(1)}, u32[]{:S(2)}, u32[]{:S(2)}) collective-permute-start(bf16[4,32,3584]{2,1,0:T(8,128)(2,1)S(1)} %broadcast_select_fusion), channel_id=1, source_target_pairs={{16,0},{17,1},{18,2},{19,3},{20,4},{21,5},{22,6},{23,7},{24,8},{25... | collective-permute-start | bytes 2752520 | tf_op jit(solution)/shard_map/ppermute | solution.py:17
Sparse Core Ops, SparseCore 0:
  67.6 25.5 reduce-scatter.1
  95.4 30.7 all-reduce.1
